TPU v7x, 256 devices: a whole 4x4x8 slice. The times are simulated.
256 devices in a mesh: ctx: 16 (over z_lo, y), dp: 16 (over x, z_hi, core).
Axes of the slice: x: 4, y: 4, z: 8 (z_hi: 2, z_lo: 4; z = z_hi * 4 + z_lo), core: 2. Of those that a mesh axis runs over, the one named last changes fastest.
Arguments:
- inputs: bfloat16 [16, 2048, 4096], P('dp', 'ctx'), may hold values from -6 to 6
- b_proj: bfloat16 [16, 2048, 512], P('dp', 'ctx'), may hold values from -0.75 to 0.75
- c_proj: bfloat16 [16, 2048, 512], P('dp', 'ctx'), may hold values from -0.75 to 0.75
- dt_raw: float32 [16, 64, 2048], P('dp', None, 'ctx'), may hold values from -3 to 9
- a_log: float32 [64], P('dp'), may hold values from -12 to -3
- dt_bias: float32 [64], P('dp'), may hold values from 0.2 to 0.8
- d_skip: float32 [64], P('dp'), may hold values from 0.5 to 1.5
- grad_out: bfloat16 [16, 2048, 4096], P('dp', 'ctx'), may hold values from -6 to 6
Outputs:
- grad_inputs: bfloat16 [16, 2048, 4096], P('dp', 'ctx')
- grad_b: bfloat16 [16, 2048, 512], P('dp', 'ctx')
- grad_c: bfloat16 [16, 2048, 512], P('dp', 'ctx')
- grad_dt: float32 [16, 64, 2048], P('dp', None, 'ctx')
- grad_alog: float32 [64], P('dp')
- grad_bias: float32 [64], P('dp')
- grad_skip: float32 [64], P('dp')
All inputs are finite; a program needn't handle non-finite values.
Results may differ from a plain program's by a relative error of at most 0.0014.
Values sent between devices are 32-bit elements; how exact they have to be, the bound alone decides.
No kernel may reach another device: no remote copies, remote signals or barrier semaphores. Data moves between devices by JAX's collectives and lax.ppermute only.
A program may use at most 192 MiB of HBM per device.

v0:
```python
import jax
import jax.numpy as jnp
from jax import lax
from jax.sharding import PartitionSpec as P

P_SIZE = 64
N = 64
G = 8
highest = lax.Precision.HIGHEST


def slab_scan(x, b, c, raw, bias, alog, skip, state_in):
    tokens, num_heads, width = x.shape
    group_heads = num_heads // G
    dt_value = jax.nn.softplus(raw + bias[:, None])
    log_decay = dt_value * (-jnp.exp(alog))[:, None]
    cumulative = jnp.cumsum(log_decay, axis=1)
    scaled = (x * dt_value.T[:, :, None]).reshape(tokens, G, group_heads, width)
    scores = jnp.einsum("qgn,kgn->gqk", c, b, precision=highest)
    offsets = jnp.arange(tokens)
    causal = offsets[:, None] >= offsets[None, :]
    spread = cumulative[:, :, None] - cumulative[:, None, :]
    weights = jnp.where(causal, jnp.exp(jnp.where(causal, spread, 0.0)), 0.0)
    mixed = weights.reshape(G, group_heads, tokens, tokens) * scores[:, None]
    local_part = jnp.einsum("gjqk,kgjp->qgjp", mixed, scaled, precision=highest)
    tail_decay = jnp.exp(cumulative[:, -1:] - cumulative)
    weighted_b = b[:, :, None, :] * tail_decay.T.reshape(tokens, G, group_heads)[:, :, :, None]
    block_state = jnp.einsum("kgjn,kgjp->gjpn", weighted_b, scaled, precision=highest)
    block_state = block_state.reshape(num_heads, width, N)
    state_out = jnp.exp(cumulative[:, -1])[:, None, None] * state_in + block_state
    entering = state_in.reshape(G, group_heads, width, N)
    cross_part = jnp.einsum("qgn,gjpn->qgjp", c, entering, precision=highest)
    cross_part = cross_part * jnp.exp(cumulative).T.reshape(tokens, G, group_heads)[:, :, :, None]
    result = (local_part + cross_part).reshape(tokens, num_heads, width)
    result = result + skip[None, :, None] * x
    return (result, state_out)


def slab_terms(x, b, c, raw, bias, alog, grad):
    tokens, num_heads, width = x.shape
    group_heads = num_heads // G
    dt_value = jax.nn.softplus(raw + bias[:, None])
    log_decay = dt_value * (-jnp.exp(alog))[:, None]
    cumulative = jnp.cumsum(log_decay, axis=1)
    total = cumulative[:, -1]
    tail_decay = jnp.exp(total[:, None] - cumulative)
    carried = (x * (dt_value * tail_decay).T[:, :, None]).reshape(tokens, G, group_heads, width)
    local_state = jnp.einsum("tgn,tgjp->gjpn", b, carried, precision=highest)
    weighted_grad = (grad * jnp.exp(cumulative).T[:, :, None]).reshape(
        tokens, G, group_heads, width
    )
    local_source = jnp.einsum("tgn,tgjp->gjpn", c, weighted_grad, precision=highest)
    return (
        total,
        local_state.reshape(num_heads, width, N),
        local_source.reshape(num_heads, width, N),
    )


def carry_across(total, local_state, local_source):
    count = lax.axis_size("ctx")
    num_heads = total.shape[0]
    share = num_heads // count
    lanes = local_state.shape[2]
    payload = jnp.concatenate(
        [local_state, local_source, jnp.broadcast_to(total[:, None, None], (num_heads, 1, lanes))],
        axis=1,
    )
    got = lax.all_to_all(payload, "ctx", 0, 0, tiled=True)
    got = got.reshape(count, share, got.shape[1], lanes)
    width = local_state.shape[1]
    states = got[:, :, :width].reshape(count, share, width * lanes)
    sources = got[:, :, width : 2 * width].reshape(count, share, width * lanes)
    totals = got[:, :, 2 * width, 0]
    slab = jnp.arange(count)
    between = (slab[None, :, None] < slab[None, None, :]) & (
        slab[None, None, :] < slab[:, None, None]
    )
    exponent = jnp.einsum("jim,mh->jih", between.astype(jnp.float32), totals, precision=highest)
    before = slab[None, :] < slab[:, None]
    chain = jnp.where(
        before[:, :, None], jnp.exp(jnp.where(before[:, :, None], exponent, 0.0)), 0.0
    )
    entering = jnp.einsum("jih,ihx->jhx", chain, states, precision=highest)
    leaving = jnp.einsum("jkh,jhx->khx", chain, sources, precision=highest)
    back = jnp.concatenate(
        [
            entering.reshape(count * share, width, lanes),
            leaving.reshape(count * share, width, lanes),
        ],
        axis=1,
    )
    mine = lax.all_to_all(back, "ctx", 0, 0, tiled=True)
    return (mine[:, :width], mine[:, width:])


def per_device(inputs, b_proj, c_proj, dt_raw, a_log, dt_bias, d_skip, grad_out):
    params = lax.all_gather(jnp.stack([a_log, dt_bias, d_skip]), "dp", axis=1, tiled=True)
    alog_all, bias_all, skip_all = (params[0], params[1], params[2])
    tokens = inputs.shape[1]
    num_heads = alog_all.shape[0]
    x = inputs[0].astype(jnp.float32).reshape(tokens, num_heads, P_SIZE)
    grad = grad_out[0].astype(jnp.float32).reshape(tokens, num_heads, P_SIZE)
    b = b_proj[0].astype(jnp.float32).reshape(tokens, G, N)
    c = c_proj[0].astype(jnp.float32).reshape(tokens, G, N)
    raw = dt_raw[0]
    total, local_state, local_source = slab_terms(x, b, c, raw, bias_all, alog_all, grad)
    entering, leaving = carry_across(total, local_state, local_source)
    _, pullback = jax.vjp(slab_scan, x, b, c, raw, bias_all, alog_all, skip_all, entering)
    gx, gb, gc, graw, gbias, galog, gskip, _ = pullback((grad, leaving))
    grad_inputs = gx.reshape(tokens, num_heads * P_SIZE).astype(jnp.bfloat16)[None]
    grad_b = gb.reshape(tokens, G * N).astype(jnp.bfloat16)[None]
    grad_c = gc.reshape(tokens, G * N).astype(jnp.bfloat16)[None]
    grad_dt = graw[None]
    head_stats = jnp.stack([galog, gbias, gskip], axis=0)
    share_size = num_heads // lax.axis_size("dp")
    summed = lax.psum(head_stats, ("ctx", "dp"))
    own_totals = lax.dynamic_slice_in_dim(summed, lax.axis_index("dp") * share_size, share_size, 1)
    return (grad_inputs, grad_b, grad_c, grad_dt, own_totals[0], own_totals[1], own_totals[2])


def solution(mesh):
    in_specs = (
        P("dp", "ctx", None),
        P("dp", "ctx", None),
        P("dp", "ctx", None),
        P("dp", None, "ctx"),
        P("dp"),
        P("dp"),
        P("dp"),
        P("dp", "ctx", None),
    )
    out_specs = (
        P("dp", "ctx", None),
        P("dp", "ctx", None),
        P("dp", "ctx", None),
        P("dp", None, "ctx"),
        P("dp"),
        P("dp"),
        P("dp"),
    )
    return jax.shard_map(
        per_device, mesh=mesh, in_specs=in_specs, out_specs=out_specs, check_vma=False
    )
```

profile of v0, /device:TPU:1, one launch (start us, length us, event | category | flops | bytes accessed | tf_op | source)
XLA Modules:
  0.0 347.0 jit_solution(9068073911150541548)
XLA Ops:
  1.5 34.5 %all-gather = f32[16,4,3]{2,1,0:T(4,128)S(1)} all-gather(f32[1,4,3]{2,1,0:T(4,128)S(1)} %bitcast.241), channel_id=1, replica_groups=mesh['ctx'=16,'dp'=16] {'dp'}, dimensions={0}, use_global_device_ids=true | all-gather | bytes 816 | tf_op jit(solution)/shard_map/all_gather | solution.py:98
  39.0 1.6 copy.188
  43.2 3.9 %fusion.9 = f32[8,8,64,64]{2,3,1,0:T(8,128)S(1)} fusion(bf16[128,8,64,1]{0,2,3,1:T(8,128)(2,1)S(1)} %bitcast.214, bf16[128,8,8,64]{0,3,2,1:T(8,128)(2,1)S(1)} %bitcast.198, f32[128,8,8]{0,2,1:T(8,128)} %bitcast.224), kind=kOutput, calls=%fused_computation.19 | convolution fusion | flops 403701760 | bytes 2260992 | tf_op jit(solution)/shard_map/tgn,tgjp->gjpn/dot_general | solution.py:52
  47.1 3.1 fusion.26
  50.5 3.2 pad_maximum_fusion
  53.6 5.7 %all-to-all-start = ((f32[64,129,64]{1,2,0:T(8,128)}), f32[64,129,64]{1,2,0:T(8,128)}, u32[]{:S(2)}, u32[]{:S(2)}) async-start(f32[64,129,64]{1,2,0:T(8,128)} %pad_maximum_fusion), calls=%async_computation | async-start | bytes 8388608 | tf_op jit(solution)/shard_map/all_to_all | solution.py:69
  59.4 78.3 %all-to-all-done = f32[64,129,64]{1,2,0:T(8,128)} async-done(((f32[64,129,64]{1,2,0:T(8,128)}), f32[64,129,64]{1,2,0:T(8,128)}, u32[]{:S(2)}, u32[]{:S(2)}) %all-to-all-start) | async-done | bytes 2113568 | tf_op jit(solution)/shard_map/all_to_all | solution.py:69
  138.7 4.9 %fusion.68 = (f32[16,4,64,64]{2,3,1,0:T(8,128)}, f32[16,4,64,64]{2,3,1,0:T(8,128)}) fusion(f32[16,4,129,64]{2,3,1,0:T(8,128)} %bitcast.26), kind=kLoop, calls=%fused_computation.110 | loop fusion | bytes 4194304 | tf_op jit(solution)/shard_map/slice | solution.py:72
  145.0 3.0 copy.200
  148.0 2.1 reshape.270
  150.1 1.8 convolution_bitcast_fusion.1
  152.6 2.4 reshape.271
  154.9 3.0 copy.204
  157.9 2.1 reshape.272
  160.0 1.8 convolution_bitcast_fusion
  162.5 2.3 reshape.273
  164.8 4.7 %pad_maximum_fusion.1 = f32[64,128,64]{2,1,0:T(8,128)} fusion(f32[64,64,64]{2,1,0:T(8,128)} %reshape.273, f32[64,64,64]{2,1,0:T(8,128)} %reshape.271), kind=kLoop, calls=%fused_computation.3 | loop fusion | flops 524288 | bytes 4194304 | tf_op jit(solution)/shard_map/concatenate | solution.py:86
  169.5 3.8 %copy.207 = f32[64,128,64]{1,2,0:T(8,128)} copy(f32[64,128,64]{2,1,0:T(8,128)} %pad_maximum_fusion.1) | data formatting | bytes 4194304 | tf_op jit(solution)/shard_map/concatenate | solution.py:86
  173.4 19.6 %all-to-all-start.1 = ((f32[64,128,64]{1,2,0:T(8,128)}), f32[64,128,64]{1,2,0:T(8,128)}, u32[]{:S(2)}, u32[]{:S(2)}) async-start(f32[64,128,64]{1,2,0:T(8,128)} %copy.207), calls=%async_computation.1 | async-start | bytes 4194304 | tf_op jit(solution)/shard_map/all_to_all | solution.py:93
  193.5 7.1 %fusion.11 = (f32[8,8,128]{2,1,0:T(8,128)S(1)}, f32[8,8,128]{2,1,0:T(8,128)}, f32[8,128,128]{1,2,0:T(8,128)}) fusion(f32[8,128,128]{1,2,0:T(8,128)S(1)} %fusion.72, f32[8,8,128]{2,1,0:T(8,128)S(1)} %bitcast.235, pred[128,128]{0,1:T(8,128)(4,1)S(1)} %iota_compare_fusion, bf16[8,8,64,128]{3,2,1,0:T(8,128)(2,1)S(1)} %bitcast.199, ...), kind=kOutput, calls=%fused_computation.21 | convolution fusion | flops 817741824 | bytes 3293184 | tf_op jit(solution)/shard_map/transpose(jvp(gjqk,kgjp->qgjp))/dot_general | solution.py:25
  201.6 6.2 %fusion.4 = f32[8,8,128,64]{2,3,1,0:T(8,128)} fusion(bf16[8,8,64,128]{3,2,1,0:T(8,128)(2,1)S(1)} %bitcast.200, f32[8,128,128]{1,2,0:T(8,128)S(1)} %fusion.72, f32[8,8,128]{2,1,0:T(8,128)S(1)} %bitcast.236, pred[128,128]{0,1:T(8,128)(4,1)S(1)} %iota_compare_fusion), kind=kOutput, calls=%fused_computation.10 | convolution fusion | flops 809500672 | bytes 3719168 | tf_op jit(solution)/shard_map/transpose(jvp(gjqk,kgjp->qgjp))/dot_general | solution.py:25
  207.8 26.7 %all-to-all-done.1 = f32[64,128,64]{1,2,0:T(8,128)} async-done(((f32[64,128,64]{1,2,0:T(8,128)}), f32[64,128,64]{1,2,0:T(8,128)}, u32[]{:S(2)}, u32[]{:S(2)}) %all-to-all-start.1) | async-done | bytes 2097184 | tf_op jit(solution)/shard_map/all_to_all | solution.py:93
  234.6 3.7 %multiply_reduce_fusion = (f32[64]{0:T(128)S(1)}, f32[64,64,64]{1,2,0:T(8,128)S(1)}, f32[64,64,64]{1,2,0:T(8,128)S(1)}) fusion(f32[64,128,64]{1,2,0:T(8,128)} %all-to-all-done.1), kind=kLoop, calls=%fused_computation.33 | loop fusion | flops 524224 | bytes 4194560 | tf_op jit(solution)/shard_map/transpose(jvp())/reduce_sum | solution.py:30
  238.3 1.8 fusion.17
  240.1 2.9 fusion.36
  243.0 3.2 fusion.19
  248.1 7.3 %multiply_reduce_fusion.1 = (f32[128,8,8]{0,2,1:T(8,128)S(1)}, f32[128,8,8,64]{0,3,2,1:T(8,128)}) fusion(f32[8,8,128,64]{2,3,1,0:T(8,128)} %fusion.4, f32[8,8,64,64]{2,3,1,0:T(8,128)} %bitcast.208, f32[128,8,8]{0,2,1:T(8,128)S(1)} %bitcast.227, f32[128,8,64]{0,2,1:T(8,128)S(1)} %convert_element_type.70, bf16[128,8,8,64]{0,3,2,1:T(8,128)(2,1)S(1)} %bitcast.206), kind=kOutput, calls=%fused_computation.34 | convolution fusion | flops 405266432 | bytes 6619136 | tf_op jit(solution)/shard_map/transpose(jvp(kgjn,kgjp->gjpn))/dot_general | solution.py:28
  256.3 2.5 fusion.16
  259.1 80.5 %psum.7 = f32[3,64]{1,0:T(4,128)S(1)} all-reduce(f32[3,64]{1,0:T(4,128)S(1)} %pad_maximum_fusion.2), channel_id=1, replica_groups=mesh['ctx'=16,'dp'=16] {'ctx','dp'}, use_global_device_ids=true, to_apply=%region_15.16 | all-reduce | flops 192 | bytes 1536 | tf_op jit(solution)/shard_map/psum | solution.py:117
  340.2 1.5 fusion.40
  342.5 1.8 fusion.39
  345.0 1.3 copy.226
  (93 shorter events, 17.3 us)
Async XLA Ops:
  0.6 40.0 %copy-start.11 = (bf16[1,128,512]{2,1,0:T(8,128)(2,1)S(1)}, bf16[1,128,512]{2,1,0:T(8,128)(2,1)}, u32[]{:S(2)}) copy-start(bf16[1,128,512]{2,1,0:T(8,128)(2,1)} %param.10) | copy-start | bytes 393220
  0.6 40.8 %copy-start.1 = (bf16[1,128,4096]{2,1,0:T(8,128)(2,1)S(1)}, bf16[1,128,4096]{2,1,0:T(8,128)(2,1)}, u32[]{:S(2)}) copy-start(bf16[1,128,4096]{2,1,0:T(8,128)(2,1)} %param.8) | copy-start | bytes 3145732
  36.2 0.9 copy-start.16
  36.2 0.9 copy-start.18
  36.2 2.8 copy-start.14
  37.5 1.5 copy-start.9
  37.6 12.6 %copy-start.12 = (f32[64]{0:T(128)}, f32[64]{0:T(128)S(1)}, u32[]{:S(2)}) copy-start(f32[64]{0:T(128)S(1)} %slice_bitcast_fusion.5) | copy-start | bytes 772
  42.2 4.9 %copy-start.8 = (f32[128,64]{0,1:T(8,128)S(1)}, f32[128,64]{0,1:T(8,128)}, u32[]{:S(2)}) copy-start(f32[128,64]{0,1:T(8,128)} %copy.194) | copy-start | bytes 98308
  53.6 84.1 %all-to-all-start = ((f32[64,129,64]{1,2,0:T(8,128)}), f32[64,129,64]{1,2,0:T(8,128)}, u32[]{:S(2)}, u32[]{:S(2)}) async-start(f32[64,129,64]{1,2,0:T(8,128)} %pad_maximum_fusion), calls=%async_computation | async-start | bytes 8388608 | tf_op jit(solution)/shard_map/all_to_all | solution.py:69
  173.4 19.6 %copy-start.6 = (f32[128,64]{1,0:T(8,128)S(1)}, f32[128,64]{1,0:T(8,128)}, u32[]{:S(2)}) copy-start(f32[128,64]{1,0:T(8,128)} %get-tuple-element.71) | copy-start | bytes 98308
  173.4 19.7 %copy-start.5 = (f32[128,64]{1,0:T(8,128)S(1)}, f32[128,64]{1,0:T(8,128)}, u32[]{:S(2)}) copy-start(f32[128,64]{1,0:T(8,128)} %get-tuple-element.73) | copy-start | bytes 98308
  173.4 20.1 %copy-start.10 = (f32[64,128]{1,0:T(8,128)S(1)}, f32[64,128]{1,0:T(8,128)}, u32[]{:S(2)}) copy-start(f32[64,128]{1,0:T(8,128)} %copy-done.9) | copy-start | bytes 98308
  173.4 61.2 %all-to-all-start.1 = ((f32[64,128,64]{1,2,0:T(8,128)}), f32[64,128,64]{1,2,0:T(8,128)}, u32[]{:S(2)}, u32[]{:S(2)}) async-start(f32[64,128,64]{1,2,0:T(8,128)} %copy.207), calls=%async_computation.1 | async-start | bytes 4194304 | tf_op jit(solution)/shard_map/all_to_all | solution.py:93
  193.1 50.0 %copy-start.3 = (f32[128,64]{0,1:T(8,128)}, f32[128,64]{0,1:T(8,128)S(1)}, u32[]{:S(2)}) copy-start(f32[128,64]{0,1:T(8,128)S(1)} %copy.212) | copy-start | bytes 98308
  238.3 4.8 %copy-start = (f32[64,64,64]{1,2,0:T(8,128)}, f32[64,64,64]{1,2,0:T(8,128)S(1)}, u32[]{:S(2)}) copy-start(f32[64,64,64]{1,2,0:T(8,128)S(1)} %get-tuple-element.67) | copy-start | bytes 3145732
  238.3 1.8 copy-start.2
  243.0 3.3 copy-start.13
  248.0 7.4 %copy-start.15 = (f32[64]{0:T(128)S(1)}, f32[64]{0:T(128)}, u32[]{:S(2)}) copy-start(f32[64]{0:T(128)} %copy-done.14) | copy-start | bytes 772
  248.0 7.4 %copy-start.19 = (f32[64]{0:T(128)S(1)}, f32[64]{0:T(128)}, u32[]{:S(2)}) copy-start(f32[64]{0:T(128)} %copy-done.18) | copy-start | bytes 772
  248.0 8.1 %copy-start.17 = (f32[64,3]{0,1:T(4,128)S(1)}, f32[64,3]{0,1:T(4,128)}, u32[]{:S(2)}) copy-start(f32[64,3]{0,1:T(4,128)} %copy-done.16) | copy-start | bytes 2308
  248.0 8.3 %copy-start.4 = (f32[128,64]{0,1:T(8,128)S(1)}, f32[128,64]{0,1:T(8,128)}, u32[]{:S(2)}) copy-start(f32[128,64]{0,1:T(8,128)} %copy-done.3) | copy-start | bytes 98308
  341.7 4.6 %copy-start.7 = (f32[64,128]{0,1:T(8,128)S(1)}, f32[64,128]{0,1:T(8,128)}, u32[]{:S(2)}) copy-start(f32[64,128]{0,1:T(8,128)} %get-tuple-element.62) | copy-start | bytes 98308
where the time goes:
time: 348 us; the launch traced here: 347 us
  blocking collectives  115 us (33%)
  waiting for transfers between devices  105 us (30%)
  matrix products  43.3 us (12%)
  local copies, waits for them, and re-layouts  38.9 us (11%)
  starting transfers between devices  25.3 us (7%)
  other arithmetic  18.2 us (5%)
    psum x1, blocking collectives, per_device(): summed = lax.psum(head_stats, ('ctx', 'dp'))  80.5 us
    all_to_all x1, waiting for transfers between devices, carry_across(): got = lax.all_to_all(payload, 'ctx', 0, 0, tiled=True)  78.3 us
    all_gather x1, blocking collectives, per_device(): lax.all_gather(jnp.stack([a_log, dt_bias, d_skip]), 'dp', axis=1, tiled=T...  34.5 us
    all_to_all x1, waiting for transfers between devices, carry_across(): mine = lax.all_to_all(back, 'ctx', 0, 0, tiled=True)  26.7 us
    all_to_all x1, starting transfers between devices, carry_across(): mine = lax.all_to_all(back, 'ctx', 0, 0, tiled=True)  19.6 us
    dot_general x2, matrix products, slab_scan(): local_part = jnp.einsum('gjqk,kgjp->qgjp', mixed, scaled, precision=highest)  13.3 us
    dot_general x2, matrix products, slab_scan(): jnp.einsum('kgjn,kgjp->gjpn', weighted_b, scaled, precision=highest)  10.5 us
    unnamed x51, local copies, waits for them, and re-layouts  8.07 us
  transfers between devices with their start and end apart: 2, of which 2 were waited for; matrix products, arithmetic and copies ran while one was open for 4% of the time, Pallas kernels for 0%

commit v1 on v0

--- a/solution.py
+++ b/solution.py
@@ -7,6 +7,12 @@
 N = 64
 G = 8
 highest = lax.Precision.HIGHEST
+
+
+def add_all(array, name):
+    parts = lax.all_gather(array, name, axis=0, tiled=False)
+    total = parts.sum(axis=0)
+    return total
 
 
 def slab_scan(x, b, c, raw, bias, alog, skip, state_in):
@@ -114,7 +120,7 @@
     grad_dt = graw[None]
     head_stats = jnp.stack([galog, gbias, gskip], axis=0)
     share_size = num_heads // lax.axis_size("dp")
-    summed = lax.psum(head_stats, ("ctx", "dp"))
+    summed = add_all(head_stats, ("ctx", "dp"))
     own_totals = lax.dynamic_slice_in_dim(summed, lax.axis_index("dp") * share_size, share_size, 1)
     return (grad_inputs, grad_b, grad_c, grad_dt, own_totals[0], own_totals[1], own_totals[2])
 

time: 348 us -> 678 us (1.95)
  the two profiles are of different devices: /device:TPU:1 before, /device:TPU:193 now
where the time goes in v1:
time: 678 us; the launch traced here: 672 us
  blocking collectives  432 us (64%)
  waiting for transfers between devices  126 us (19%)
  matrix products  42.3 us (6%)
  local copies, waits for them, and re-layouts  38.9 us (6%)
  other arithmetic  18.5 us (3%)
  starting transfers between devices  13 us (2%)
    all_gather x1, blocking collectives, add_all(): parts = lax.all_gather(array, name, axis=0, tiled=False)  407 us
    all_to_all x1, waiting for transfers between devices, carry_across(): got = lax.all_to_all(payload, 'ctx', 0, 0, tiled=True)  93.1 us
    all_to_all x1, waiting for transfers between devices, carry_across(): mine = lax.all_to_all(back, 'ctx', 0, 0, tiled=True)  32.4 us
    all_gather x1, blocking collectives, per_device(): lax.all_gather(jnp.stack([a_log, dt_bias, d_skip]), 'dp', axis=1, tiled=T...  24.9 us
  transfers between devices with their start and end apart: 2, of which 2 were waited for; matrix products, arithmetic and copies ran while one was open for 2% of the time, Pallas kernels for 0%

profile of v1, /device:TPU:193, one launch (start us, length us, event | category | flops | bytes accessed | tf_op | source)
XLA Modules:
  0.0 671.5 jit_solution(7891102443150185500)
XLA Ops:
  1.5 24.9 %all-gather.1 = f32[16,4,3]{2,1,0:T(4,128)S(1)} all-gather(f32[1,4,3]{2,1,0:T(4,128)S(1)} %bitcast.243), channel_id=1, replica_groups=mesh['ctx'=16,'dp'=16] {'dp'}, dimensions={0}, use_global_device_ids=true | all-gather | bytes 816 | tf_op jit(solution)/shard_map/all_gather | solution.py:104
  29.4 1.6 copy.188
  33.6 3.9 fusion.9
  37.5 3.1 fusion.26
  40.9 3.2 pad_maximum_fusion
  44.1 8.3 %all-to-all-start = ((f32[64,129,64]{1,2,0:T(8,128)}), f32[64,129,64]{1,2,0:T(8,128)}, u32[]{:S(2)}, u32[]{:S(2)}) async-start(f32[64,129,64]{1,2,0:T(8,128)} %pad_maximum_fusion), calls=%async_computation | async-start | bytes 8388608 | tf_op jit(solution)/shard_map/all_to_all | solution.py:75
  52.3 93.1 %all-to-all-done = f32[64,129,64]{1,2,0:T(8,128)} async-done(((f32[64,129,64]{1,2,0:T(8,128)}), f32[64,129,64]{1,2,0:T(8,128)}, u32[]{:S(2)}, u32[]{:S(2)}) %all-to-all-start) | async-done | bytes 2113568 | tf_op jit(solution)/shard_map/all_to_all | solution.py:75
  146.4 4.9 fusion.68
  152.7 3.0 copy.200
  155.6 2.1 reshape.270
  157.8 1.8 convolution_bitcast_fusion.1
  160.3 2.4 reshape.271
  162.6 3.0 copy.204
  165.6 2.1 reshape.272
  167.7 1.8 convolution_bitcast_fusion
  170.2 2.3 reshape.273
  172.5 4.7 pad_maximum_fusion.1
  177.2 3.8 copy.207
  181.0 4.7 all-to-all-start.1
  186.3 7.1 %fusion.11 = (f32[8,8,128]{2,1,0:T(8,128)S(1)}, f32[8,8,128]{2,1,0:T(8,128)}, f32[8,128,128]{1,2,0:T(8,128)}) fusion(f32[8,128,128]{1,2,0:T(8,128)S(1)} %fusion.72, f32[8,8,128]{2,1,0:T(8,128)S(1)} %bitcast.237, pred[128,128]{0,1:T(8,128)(4,1)S(1)} %iota_compare_fusion, bf16[8,8,64,128]{3,2,1,0:T(8,128)(2,1)S(1)} %bitcast.201, ...), kind=kOutput, calls=%fused_computation.21 | convolution fusion | flops 817741824 | bytes 3293184 | tf_op jit(solution)/shard_map/transpose(jvp(gjqk,kgjp->qgjp))/dot_general | solution.py:31
  194.4 6.3 fusion.4
  200.7 32.4 %all-to-all-done.1 = f32[64,128,64]{1,2,0:T(8,128)} async-done(((f32[64,128,64]{1,2,0:T(8,128)}), f32[64,128,64]{1,2,0:T(8,128)}, u32[]{:S(2)}, u32[]{:S(2)}) %all-to-all-start.1) | async-done | bytes 2097184 | tf_op jit(solution)/shard_map/all_to_all | solution.py:99
  233.2 3.7 multiply_reduce_fusion
  236.9 1.8 fusion.17
  238.7 2.9 fusion.36
  241.6 3.2 fusion.19
  245.3 1.3 reduce_window_sum.25
  246.7 7.3 %multiply_reduce_fusion.1 = (f32[128,8,8]{0,2,1:T(8,128)S(1)}, f32[128,8,8,64]{0,3,2,1:T(8,128)}) fusion(f32[8,8,128,64]{2,3,1,0:T(8,128)} %fusion.4, f32[8,8,64,64]{2,3,1,0:T(8,128)} %bitcast.210, f32[128,8,8]{0,2,1:T(8,128)S(1)} %bitcast.229, f32[128,8,64]{0,2,1:T(8,128)S(1)} %convert_element_type.70, bf16[128,8,8,64]{0,3,2,1:T(8,128)(2,1)S(1)} %bitcast.208), kind=kOutput, calls=%fused_computation.34 | convolution fusion | flops 405266432 | bytes 6619136 | tf_op jit(solution)/shard_map/transpose(jvp(kgjn,kgjp->gjpn))/dot_general | solution.py:34
  254.9 2.5 fusion.16
  257.7 407.0 %all-gather.2 = f32[256,3,64]{2,1,0:T(4,128)S(1)} all-gather(f32[1,3,64]{2,1,0:T(4,128)S(1)} %maximum_bitcast_fusion.1), channel_id=2, replica_groups=mesh['ctx'=16,'dp'=16] {'ctx','dp'}, dimensions={0}, use_global_device_ids=true | all-gather | bytes 197376 | tf_op jit(solution)/shard_map/all_gather | solution.py:13
  665.6 1.5 fusion.40
  669.3 1.3 copy.226
  (98 shorter events, 17.0 us)
Async XLA Ops:
  0.6 30.4 %copy-start.13 = (bf16[1,128,512]{2,1,0:T(8,128)(2,1)S(1)}, bf16[1,128,512]{2,1,0:T(8,128)(2,1)}, u32[]{:S(2)}) copy-start(bf16[1,128,512]{2,1,0:T(8,128)(2,1)} %param.10) | copy-start | bytes 393220
  0.6 31.3 %copy-start.3 = (bf16[1,128,4096]{2,1,0:T(8,128)(2,1)S(1)}, bf16[1,128,4096]{2,1,0:T(8,128)(2,1)}, u32[]{:S(2)}) copy-start(bf16[1,128,4096]{2,1,0:T(8,128)(2,1)} %param.8) | copy-start | bytes 3145732
  26.6 0.9 copy-start.18
  26.6 0.9 copy-start.20
  26.6 2.8 copy-start.16
  27.9 1.5 copy-start.11
  28.0 12.6 %copy-start.14 = (f32[64]{0:T(128)}, f32[64]{0:T(128)S(1)}, u32[]{:S(2)}) copy-start(f32[64]{0:T(128)S(1)} %slice_bitcast_fusion.5) | copy-start | bytes 772
  32.6 4.9 copy-start.10
  44.1 101.3 %all-to-all-start = ((f32[64,129,64]{1,2,0:T(8,128)}), f32[64,129,64]{1,2,0:T(8,128)}, u32[]{:S(2)}, u32[]{:S(2)}) async-start(f32[64,129,64]{1,2,0:T(8,128)} %pad_maximum_fusion), calls=%async_computation | async-start | bytes 8388608 | tf_op jit(solution)/shard_map/all_to_all | solution.py:75
  181.0 4.7 copy-start.8
  181.0 4.8 copy-start.7
  181.0 5.2 copy-start.12
  181.0 52.2 %all-to-all-start.1 = ((f32[64,128,64]{1,2,0:T(8,128)}), f32[64,128,64]{1,2,0:T(8,128)}, u32[]{:S(2)}, u32[]{:S(2)}) async-start(f32[64,128,64]{1,2,0:T(8,128)} %copy.207), calls=%async_computation.1 | async-start | bytes 4194304 | tf_op jit(solution)/shard_map/all_to_all | solution.py:99
  185.8 55.8 %copy-start.5 = (f32[128,64]{0,1:T(8,128)}, f32[128,64]{0,1:T(8,128)S(1)}, u32[]{:S(2)}) copy-start(f32[128,64]{0,1:T(8,128)S(1)} %copy.212) | copy-start | bytes 98308
  236.9 4.8 copy-start
  236.9 1.8 copy-start.4
  241.6 3.3 copy-start.15
  246.6 7.4 %copy-start.17 = (f32[64]{0:T(128)S(1)}, f32[64]{0:T(128)}, u32[]{:S(2)}) copy-start(f32[64]{0:T(128)} %copy-done.16) | copy-start | bytes 772
  246.6 7.4 %copy-start.21 = (f32[64]{0:T(128)S(1)}, f32[64]{0:T(128)}, u32[]{:S(2)}) copy-start(f32[64]{0:T(128)} %copy-done.20) | copy-start | bytes 772
  246.6 8.1 %copy-start.19 = (f32[64,3]{0,1:T(4,128)S(1)}, f32[64,3]{0,1:T(4,128)}, u32[]{:S(2)}) copy-start(f32[64,3]{0,1:T(4,128)} %copy-done.18) | copy-start | bytes 2308
  246.7 8.2 %copy-start.6 = (f32[128,64]{0,1:T(8,128)S(1)}, f32[128,64]{0,1:T(8,128)}, u32[]{:S(2)}) copy-start(f32[128,64]{0,1:T(8,128)} %copy-done.5) | copy-start | bytes 98308
  257.4 410.4 %copy-start.1 = (f32[8,128,128]{1,2,0:T(8,128)S(1)}, f32[8,128,128]{1,2,0:T(8,128)}, u32[]{:S(2)}) copy-start(f32[8,128,128]{1,2,0:T(8,128)} %get-tuple-element.58) | copy-start | bytes 1572868
  257.4 410.4 %copy-start.2 = (f32[128,8,64]{0,2,1:T(8,128)S(1)}, f32[128,8,64]{0,2,1:T(8,128)}, u32[]{:S(2)}) copy-start(f32[128,8,64]{0,2,1:T(8,128)} %get-tuple-element.60) | copy-start | bytes 786436
  667.1 3.5 copy-start.9
